TPU v7x, 512 devices: a whole 4x8x8 slice. The times are simulated.
512 devices in a mesh: gx: 32 (over z, y_hi, core), gy: 16 (over x, y_lo).
Axes of the slice: x: 4, y: 8 (y_hi: 2, y_lo: 4; y = y_hi * 4 + y_lo), z: 8, core: 2. Of those that a mesh axis runs over, the one named last changes fastest.
Arguments:
- design: float32 [256, 128, 128], P('gx', 'gy'), may hold values from 0.06 to 0.9
- passive: int32 [256, 128, 128], P('gx', 'gy'), may hold values 0 or 1
- basis_pairs: float32 [4, 2, 3, 256, 128, 128], P(None, None, None, 'gx', 'gy'), may hold values from -6 to 6
- supports: int32 [256, 128, 128], P('gx', 'gy'), may hold values 0 or 1
- stiffness: float32 [24, 24], replicated, may hold values from -1.25 to 1.25
- mass_matrix: float32 [24, 24], replicated, may hold values from -1.25 to 1.25
- volume_fraction: float32 [64], replicated, may hold values from 0.26 to 0.36
Outputs:
- sensitivity: float32 [256, 128, 128], P('gx', 'gy')
- design_next: float32 [256, 128, 128], P('gx', 'gy')
All inputs are finite; a program needn't handle non-finite values. No bound on the sum of `passive` or of `supports` on one device may be relied on, other than what follows from the above.
Results may differ from a plain program's by a relative error of at most 0.0003.
Values sent between devices are 32-bit elements; how exact they have to be, the bound alone decides.
No kernel may reach another device: no remote copies, remote signals or barrier semaphores. Data moves between devices by JAX's collectives and lax.ppermute only.
A program may use at most 64 MiB of HBM per device.

v0:
```python
import math
import jax
import jax.numpy as jnp
from jax import lax
from jax.sharding import PartitionSpec as P

BISECT = 6
REGIONS = 64
PENALTY_SCALE = 3.0 * (1.0 - 0.001)
OMEGA_SQUARED = 0.5
MOVE_LIMIT = 0.2


def with_halo(cells, sides, width):
    for axis, dim in sides:
        count = lax.axis_size(axis)
        ends = count - 1
        head = lax.slice_in_dim(cells, 0, width, axis=dim)
        tail = lax.slice_in_dim(cells, cells.shape[dim] - width, cells.shape[dim], axis=dim)
        cells = jnp.concatenate(
            [
                lax.ppermute(tail, axis, [(i, (i + 1) % count) for i in range(ends)]),
                cells,
                lax.ppermute(head, axis, [((i + 1) % count, i) for i in range(ends)]),
            ],
            axis=dim,
        )
    return cells


def from_behind(value, axis, steps):
    count = lax.axis_size(axis)
    initial, last = (max(0, -steps), min(count, count - steps))
    return lax.ppermute(value, axis, [(source, source + steps) for source in range(initial, last)])


def filter_taps():
    tap_list = []
    for offset_x in range(-2, 3):
        for offset_y in range(-2, 3):
            for offset_z in range(-2, 3):
                weight = 3.0 - math.sqrt(
                    offset_x * offset_x + offset_y * offset_y + offset_z * offset_z
                )
                if weight > 0.0:
                    tap_list.append((offset_x, offset_y, offset_z, weight))
    return tap_list


def stencil(padded, block_shape):
    result = jnp.zeros(block_shape, jnp.float32)
    for offset_x, offset_y, offset_z, weight in filter_taps():
        result = (
            result
            + weight
            * padded[
                2 + offset_x : 2 + offset_x + block_shape[0],
                2 + offset_y : 2 + offset_y + block_shape[1],
                2 + offset_z : 2 + offset_z + block_shape[2],
            ]
        )
    return result


def element_terms(extended, stiffness, mass_matrix):
    pair_count = extended.shape[0]
    cells_x = extended.shape[3] - 1
    cells_y = extended.shape[4] - 1
    cells_z = extended.shape[5] - 1
    stiff_energy = jnp.zeros((cells_x * cells_y * cells_z,), jnp.float32)
    mass_energy = jnp.zeros((cells_x * cells_y * cells_z,), jnp.float32)
    for pair_index in range(pair_count):
        vectors = []
        for member in range(2):
            row_list = []
            for corner_x in (0, 1):
                for corner_y in (0, 1):
                    for corner_z in (0, 1):
                        for component in range(3):
                            row_list.append(
                                extended[
                                    pair_index,
                                    member,
                                    component,
                                    corner_x : corner_x + cells_x,
                                    corner_y : corner_y + cells_y,
                                    corner_z : corner_z + cells_z,
                                ].reshape(-1)
                            )
            vectors.append(jnp.stack(row_list))
        state_rows, adjoint_rows = vectors
        stiff_energy = stiff_energy + jnp.sum(
            state_rows * jnp.dot(stiffness, adjoint_rows, precision=lax.Precision.HIGHEST), axis=0
        )
        mass_energy = mass_energy + jnp.sum(
            state_rows * jnp.dot(mass_matrix, adjoint_rows, precision=lax.Precision.HIGHEST), axis=0
        )
    return (
        stiff_energy.reshape(cells_x, cells_y, cells_z),
        mass_energy.reshape(cells_x, cells_y, cells_z),
    )


def shards(design, passive, basis_pairs, supports, stiffness, mass_matrix, volume_fraction):
    block_shape = design.shape
    size_x, size_y, size_z = block_shape
    devices_x = lax.axis_size("gx")
    devices_y = lax.axis_size("gy")
    index_x = lax.axis_index("gx")
    index_y = lax.axis_index("gy")
    grid_x = size_x * devices_x
    grid_y = size_y * devices_y
    spread_x = jnp.arange(size_x + 4, dtype=jnp.int32) + index_x * size_x - 2
    spread_y = jnp.arange(size_y + 4, dtype=jnp.int32) + index_y * size_y - 2
    valid_x = ((spread_x >= 0) & (spread_x < grid_x)).astype(jnp.float32)
    valid_y = ((spread_y >= 0) & (spread_y < grid_y)).astype(jnp.float32)
    valid_z = jnp.pad(jnp.ones((size_z,), jnp.float32), 2)
    inside = valid_x[:, None, None] * valid_y[None, :, None] * valid_z[None, None, :]
    weight_sum = stencil(inside, block_shape)
    design_wide = with_halo(design, (("gx", 0), ("gy", 1)), 2)
    design_wide = jnp.pad(design_wide, ((0, 0), (0, 0), (2, 2)))
    physical = jnp.where(passive == 1, 1.0, stencil(design_wide, block_shape) / weight_sum)
    fields = basis_pairs * (1 - supports).astype(jnp.float32)
    rim_first = from_behind(fields[:, :, :, :1], "gx", -1)
    widened = jnp.concatenate([fields, rim_first], axis=3)
    rim_second = from_behind(widened[:, :, :, :, :1], "gy", -1)
    extended = jnp.concatenate([widened, rim_second], axis=4)
    extended = jnp.pad(extended, ((0, 0), (0, 0), (0, 0), (0, 0), (0, 0), (0, 1)))
    stiff_energy, mass_energy = element_terms(extended, stiffness, mass_matrix)
    raw_sensitivity = -(
        PENALTY_SCALE * physical * physical * stiff_energy - OMEGA_SQUARED * mass_energy
    )
    raw_sensitivity = jnp.where(passive == 1, 0.0, raw_sensitivity)
    scaled_wide = with_halo(raw_sensitivity / weight_sum, (("gx", 0), ("gy", 1)), 2)
    scaled_wide = jnp.pad(scaled_wide, ((0, 0), (0, 0), (2, 2)))
    sensitivity = stencil(scaled_wide, block_shape)
    benefit = jnp.maximum(-sensitivity, 0.0)
    floor_value = jnp.maximum(design - MOVE_LIMIT, 0.0)
    ceiling = jnp.minimum(design + MOVE_LIMIT, 1.0)
    band_cells = size_z // REGIONS
    target = volume_fraction * float(grid_x * grid_y * band_cells)

    def candidate(multiplier):
        per_cell = jnp.repeat(multiplier, band_cells)[None, None, :]
        trial = design * jnp.sqrt(benefit / per_cell)
        return jnp.where(passive == 1, 1.0, jnp.minimum(ceiling, jnp.maximum(floor_value, trial)))

    def region_sum(field):
        return jnp.sum(field, axis=(0, 1)).reshape(REGIONS, band_cells).sum(axis=1)

    levels = BISECT

    def bisect_round(round_index, bracket):
        low_end, high_end = bracket
        level_nodes = [(low_end, high_end)]
        midpoints = []
        for depth in range(levels):
            next_nodes = []
            for node_low, node_high in level_nodes:
                middle = jnp.sqrt(node_low * node_high)
                midpoints.append(middle)
                next_nodes.append((node_low, middle))
                next_nodes.append((middle, node_high))
            level_nodes = next_nodes
        trial_multipliers = jnp.stack(midpoints)
        per_cell = jnp.repeat(trial_multipliers, band_cells, axis=1)[:, None, None, :]
        trial = design[None] * jnp.sqrt(benefit[None] / per_cell)
        fields_of = jnp.where(
            passive[None] == 1,
            1.0,
            jnp.minimum(ceiling[None], jnp.maximum(floor_value[None], trial)),
        )
        partial_volumes = (
            jnp.sum(fields_of, axis=(1, 2)).reshape(len(midpoints), REGIONS, band_cells).sum(axis=2)
        )
        volumes = lax.psum(partial_volumes, ("gx", "gy"))
        position = jnp.zeros((REGIONS,), jnp.int32)
        for depth in range(levels):
            middle = jnp.sqrt(low_end * high_end)
            heap_index = position + (2**depth - 1)
            chosen = jnp.take_along_axis(volumes, heap_index[None, :], axis=0)[0]
            heavier = chosen > target
            low_end = jnp.where(heavier, middle, low_end)
            high_end = jnp.where(heavier, high_end, middle)
            position = 2 * position + heavier.astype(jnp.int32)
        return (low_end, high_end)

    start = (jnp.full((REGIONS,), 0.0001, jnp.float32), jnp.full((REGIONS,), 10000.0, jnp.float32))
    low_end, high_end = bisect_round(0, start)
    design_next = candidate(jnp.sqrt(low_end * high_end))
    return (sensitivity, design_next)


def solution(mesh):
    placed = (
        P("gx", "gy", None),
        P("gx", "gy", None),
        P(None, None, None, "gx", "gy", None),
        P("gx", "gy", None),
        P(),
        P(),
        P(),
    )
    return jax.shard_map(
        shards,
        mesh=mesh,
        in_specs=placed,
        out_specs=(P("gx", "gy", None), P("gx", "gy", None)),
        check_vma=False,
    )
```

profile of v0, /device:TPU:1, one launch (start us, length us, event | category | flops | bytes accessed | tf_op | source)
XLA Modules:
  0.0 233.9 jit_solution(4660837941216454200)
XLA Ops:
  1.4 8.8 %collective-permute-start.1 = (f32[2,8,128]{2,1,0:T(8,128)S(1)}, f32[2,8,128]{2,1,0:T(8,128)S(1)}, u32[]{:S(2)}, u32[]{:S(2)}) collective-permute-start(f32[2,8,128]{2,1,0:T(8,128)S(1)} %get-tuple-element.214), channel_id=1, source_target_pairs={{16,0},{32,16},{48,32},{64,48},{80,64},{96,80},{112,96},{128,112},... | collective-permute-start | bytes 24584 | tf_op jit(solution)/shard_map/ppermute | solution.py:24
  10.2 2.0 collective-permute-start
  13.0 1.2 broadcast_multiply_fusion
  14.2 2.3 %collective-permute-start.4 = (f32[4,2,3,1,8,128]{5,4,3,2,1,0:T(8,128)S(1)}, f32[4,2,3,1,8,128]{5,4,3,2,1,0:T(8,128)S(1)}, u32[]{:S(2)}, u32[]{:S(2)}) collective-permute-start(f32[4,2,3,1,8,128]{5,4,3,2,1,0:T(8,128)S(1)} %slice.2424), channel_id=1, source_target_pairs={{16,0},{32,16},{48,32},{64,48},{80,64},{96,80},{112,96},{128,112},... | collective-permute-start | bytes 294920 | tf_op jit(solution)/shard_map/ppermute | solution.py:34
  18.3 2.3 collective-permute-start.2
  20.6 1.3 collective-permute-start.3
  22.4 2.7 %collective-permute-done.3 = f32[12,2,128]{2,1,0:T(2,128)S(1)} collective-permute-done((f32[12,2,128]{2,1,0:T(2,128)S(1)}, f32[12,2,128]{2,1,0:T(2,128)S(1)}, u32[]{:S(2)}, u32[]{:S(2)}) %collective-permute-start.3) | collective-permute-done | bytes 12320 | tf_op jit(solution)/shard_map/ppermute | solution.py:24
  25.4 1.3 collective-permute-start.5
  29.0 4.9 %collective-permute-done.5 = f32[4,2,3,9,1,128]{5,3,4,2,1,0:T(8,128)S(1)} collective-permute-done((f32[4,2,3,9,1,128]{5,3,4,2,1,0:T(8,128)S(1)}, f32[4,2,3,9,1,128]{5,3,4,2,1,0:T(8,128)S(1)}, u32[]{:S(2)}, u32[]{:S(2)}) %collective-permute-start.5) | collective-permute-done | bytes 110624 | tf_op jit(solution)/shard_map/ppermute | solution.py:34
  35.1 1.0 pad_slice_fusion.79
  36.1 1.1 pad_slice_fusion.48
  38.0 1.1 fusion.373
  40.0 3.7 %stack.24 = f32[24,8192]{1,0:T(8,128)S(1)} concatenate(f32[1,8192]{1,0:T(1,128)} %bitcast.576, f32[1,8192]{1,0:T(1,128)} %bitcast.575, f32[1,8192]{1,0:T(1,128)} %bitcast.574, f32[1,8192]{1,0:T(1,128)} %bitcast.624, f32[1,8192]{1,0:T(1,128)} %bitcast.497, f32[1,8192]{1,0:T(1,128)} %bitcast.498, f32[1,8192]{1,0:T(1,128)} %bitcast.623, f32[1,8192]{1,0:T(1,128)} %bitcast.622, ...), dimensions={0} | concatenate | bytes 1572864 | tf_op jit(solution)/shard_map/stack | solution.py:90
  43.8 5.8 %stack.25 = f32[24,8192]{1,0:T(8,128)} concatenate(f32[1,8192]{1,0:T(1,128)} %bitcast.571, f32[1,8192]{1,0:T(1,128)} %bitcast.570, f32[1,8192]{1,0:T(1,128)} %bitcast.588, f32[1,8192]{1,0:T(1,128)} %bitcast.468, f32[1,8192]{1,0:T(1,128)} %bitcast.469, f32[1,8192]{1,0:T(1,128)} %bitcast.470, f32[1,8192]{1,0:T(1,128)} %bitcast.617, f32[1,8192]{1,0:T(1,128)} %bitcast.616, ...), dimensions={0} | concatenate | bytes 1572864 | tf_op jit(solution)/shard_map/stack | solution.py:90
  49.6 2.7 %fusion.17 = f32[8192]{0:T(1024)} fusion(f32[24,8192]{1,0:T(8,128)S(1)} %stack.24, f32[24,8192]{1,0:T(8,128)} %stack.25, f32[24,24]{1,0:T(8,128)S(1)} %copy-done), kind=kOutput, calls=%fused_computation.153 | convolution fusion | flops 57008128 | bytes 1607936 | tf_op jit(solution)/shard_map/dot_general | solution.py:96
  52.3 1.5 fusion.13
  53.8 3.7 %stack.31 = f32[24,8192]{1,0:T(8,128)S(1)} concatenate(f32[1,8192]{1,0:T(1,128)} %bitcast.564, f32[1,8192]{1,0:T(1,128)} %bitcast.584, f32[1,8192]{1,0:T(1,128)} %bitcast.580, f32[1,8192]{1,0:T(1,128)} %bitcast.514, f32[1,8192]{1,0:T(1,128)} %bitcast.515, f32[1,8192]{1,0:T(1,128)} %bitcast.516, f32[1,8192]{1,0:T(1,128)} %bitcast.531, f32[1,8192]{1,0:T(1,128)} %bitcast.530, ...), dimensions={0} | concatenate | bytes 1572864 | tf_op jit(solution)/shard_map/stack | solution.py:90
  57.5 5.8 %stack.30 = f32[24,8192]{1,0:T(8,128)} concatenate(f32[1,8192]{1,0:T(1,128)} %bitcast.558, f32[1,8192]{1,0:T(1,128)} %bitcast.557, f32[1,8192]{1,0:T(1,128)} %bitcast.556, f32[1,8192]{1,0:T(1,128)} %bitcast.466, f32[1,8192]{1,0:T(1,128)} %bitcast.479, f32[1,8192]{1,0:T(1,128)} %bitcast.480, f32[1,8192]{1,0:T(1,128)} %bitcast.513, f32[1,8192]{1,0:T(1,128)} %bitcast.512, ...), dimensions={0} | concatenate | bytes 1572864 | tf_op jit(solution)/shard_map/stack | solution.py:90
  63.3 2.7 %fusion.20 = f32[8192]{0:T(1024)} fusion(f32[24,8192]{1,0:T(8,128)} %stack.30, f32[24,8192]{1,0:T(8,128)S(1)} %stack.31, f32[24,24]{1,0:T(8,128)S(1)} %copy-done), kind=kOutput, calls=%fused_computation.156 | convolution fusion | flops 57008128 | bytes 1607936 | tf_op jit(solution)/shard_map/dot_general | solution.py:96
  66.0 1.5 fusion.16
  69.5 3.7 %stack.27 = f32[24,8192]{1,0:T(8,128)S(1)} concatenate(f32[1,8192]{1,0:T(1,128)} %bitcast.569, f32[1,8192]{1,0:T(1,128)} %bitcast.568, f32[1,8192]{1,0:T(1,128)} %bitcast.567, f32[1,8192]{1,0:T(1,128)} %bitcast.534, f32[1,8192]{1,0:T(1,128)} %bitcast.535, f32[1,8192]{1,0:T(1,128)} %bitcast.536, f32[1,8192]{1,0:T(1,128)} %bitcast.610, f32[1,8192]{1,0:T(1,128)} %bitcast.609, ...), dimensions={0} | concatenate | bytes 1572864 | tf_op jit(solution)/shard_map/stack | solution.py:90
  73.3 3.6 %stack.26 = f32[24,8192]{1,0:T(8,128)S(1)} concatenate(f32[1,8192]{1,0:T(1,128)S(1)} %bitcast.563, f32[1,8192]{1,0:T(1,128)S(1)} %bitcast.562, f32[1,8192]{1,0:T(1,128)S(1)} %bitcast.561, f32[1,8192]{1,0:T(1,128)S(1)} %bitcast.450, f32[1,8192]{1,0:T(1,128)S(1)} %bitcast.451, f32[1,8192]{1,0:T(1,128)S(1)} %bitcast.452, f32[1,8192]{1,0:T(1,128)} %bitcast.611, f32[1,8192]{1,0:T(1,128)} %bitcast.607, ...), dimensions={0} | concatenate | bytes 1572864 | tf_op jit(solution)/shard_map/stack | solution.py:90
  79.0 3.4 %stack.29 = f32[24,8192]{1,0:T(8,128)S(1)} concatenate(f32[1,8192]{1,0:T(1,128)S(1)} %bitcast.549, f32[1,8192]{1,0:T(1,128)S(1)} %bitcast.548, f32[1,8192]{1,0:T(1,128)S(1)} %bitcast.547, f32[1,8192]{1,0:T(1,128)S(1)} %bitcast.438, f32[1,8192]{1,0:T(1,128)S(1)} %bitcast.439, f32[1,8192]{1,0:T(1,128)S(1)} %bitcast.440, f32[1,8192]{1,0:T(1,128)} %bitcast.602, f32[1,8192]{1,0:T(1,128)} %bitcast.601, ...), dimensions={0} | concatenate | bytes 1572864 | tf_op jit(solution)/shard_map/stack | solution.py:90
  82.5 1.2 stack.28
  85.5 1.2 fusion.98
  86.8 8.2 %collective-permute-start.6 = (f32[2,8,128]{2,1,0:T(8,128)S(1)}, f32[2,8,128]{2,1,0:T(8,128)S(1)}, u32[]{:S(2)}, u32[]{:S(2)}) collective-permute-start(f32[2,8,128]{2,1,0:T(8,128)S(1)} %get-tuple-element.212), channel_id=1, source_target_pairs={{0,16},{16,32},{32,48},{48,64},{64,80},{80,96},{96,112},{112,128},... | collective-permute-start | bytes 24584 | tf_op jit(solution)/shard_map/ppermute | solution.py:22
  94.9 1.9 collective-permute-start.7
  96.9 6.9 %collective-permute-done.7 = f32[2,8,128]{2,1,0:T(8,128)S(1)} collective-permute-done((f32[2,8,128]{2,1,0:T(8,128)S(1)}, f32[2,8,128]{2,1,0:T(8,128)S(1)}, u32[]{:S(2)}, u32[]{:S(2)}) %collective-permute-start.7) | collective-permute-done | bytes 8224 | tf_op jit(solution)/shard_map/ppermute | solution.py:24
  103.8 3.1 %collective-permute-start.8 = (f32[12,2,128]{2,1,0:T(2,128)S(1)}, f32[12,2,128]{2,1,0:T(2,128)S(1)}, u32[]{:S(2)}, u32[]{:S(2)}) collective-permute-start(f32[12,2,128]{2,1,0:T(2,128)S(1)} %get-tuple-element.203), channel_id=1, source_target_pairs={{0,1},{1,2},{2,3},{3,4},{4,5},{5,6},{6,7},{7,8},{8,9},{9,10},{10,1... | collective-permute-start | bytes 36872 | tf_op jit(solution)/shard_map/ppermute | solution.py:22
  106.9 1.3 collective-permute-start.9
  108.4 5.7 %collective-permute-done.9 = f32[12,2,128]{2,1,0:T(2,128)S(1)} collective-permute-done((f32[12,2,128]{2,1,0:T(2,128)S(1)}, f32[12,2,128]{2,1,0:T(2,128)S(1)}, u32[]{:S(2)}, u32[]{:S(2)}) %collective-permute-start.9) | collective-permute-done | bytes 12320 | tf_op jit(solution)/shard_map/ppermute | solution.py:24
  116.1 111.8 %psum.7 = f32[63,64]{1,0:T(8,128)S(1)} all-reduce(f32[63,64]{1,0:T(8,128)S(1)} %copy.118), channel_id=1, replica_groups=mesh['gx'=32,'gy'=16] {'gx','gy'}, use_global_device_ids=true, to_apply=%region_10.11 | all-reduce | flops 4032 | bytes 32256 | tf_op jit(solution)/shard_map/psum | solution.py:176
  (198 shorter events, 22.7 us)
Async XLA Ops:
  0.6 49.0 %copy-start = (f32[24,24]{1,0:T(8,128)S(1)}, f32[24,24]{1,0:T(8,128)}, u32[]{:S(2)}) copy-start(f32[24,24]{1,0:T(8,128)} %param.14) | copy-start | bytes 6916
  0.6 17.0 %copy-start.3 = (f32[8,8,128]{2,1,0:T(8,128)S(1)}, f32[8,8,128]{2,1,0:T(8,128)}, u32[]{:S(2)}) copy-start(f32[8,8,128]{2,1,0:T(8,128)} %param.9) | copy-start | bytes 98308
  1.4 16.8 %collective-permute-start.1 = (f32[2,8,128]{2,1,0:T(8,128)S(1)}, f32[2,8,128]{2,1,0:T(8,128)S(1)}, u32[]{:S(2)}, u32[]{:S(2)}) collective-permute-start(f32[2,8,128]{2,1,0:T(8,128)S(1)} %get-tuple-element.214), channel_id=1, source_target_pairs={{16,0},{32,16},{48,32},{64,48},{80,64},{96,80},{112,96},{128,112},... | collective-permute-start | bytes 24584 | tf_op jit(solution)/shard_map/ppermute | solution.py:24
  10.2 7.4 %collective-permute-start = (f32[2,8,128]{2,1,0:T(8,128)S(1)}, f32[2,8,128]{2,1,0:T(8,128)S(1)}, u32[]{:S(2)}, u32[]{:S(2)}) collective-permute-start(f32[2,8,128]{2,1,0:T(8,128)S(1)} %get-tuple-element.215), channel_id=1, source_target_pairs={{0,16},{16,32},{32,48},{48,64},{64,80},{80,96},{96,112},{112,128},... | collective-permute-start | bytes 24584 | tf_op jit(solution)/shard_map/ppermute | solution.py:22
  14.2 11.1 %collective-permute-start.4 = (f32[4,2,3,1,8,128]{5,4,3,2,1,0:T(8,128)S(1)}, f32[4,2,3,1,8,128]{5,4,3,2,1,0:T(8,128)S(1)}, u32[]{:S(2)}, u32[]{:S(2)}) collective-permute-start(f32[4,2,3,1,8,128]{5,4,3,2,1,0:T(8,128)S(1)} %slice.2424), channel_id=1, source_target_pairs={{16,0},{32,16},{48,32},{64,48},{80,64},{96,80},{112,96},{128,112},... | collective-permute-start | bytes 294920 | tf_op jit(solution)/shard_map/ppermute | solution.py:34
  18.3 4.1 %collective-permute-start.2 = (f32[12,2,128]{2,1,0:T(2,128)S(1)}, f32[12,2,128]{2,1,0:T(2,128)S(1)}, u32[]{:S(2)}, u32[]{:S(2)}) collective-permute-start(f32[12,2,128]{2,1,0:T(2,128)S(1)} %get-tuple-element.205), channel_id=1, source_target_pairs={{0,1},{1,2},{2,3},{3,4},{4,5},{5,6},{6,7},{7,8},{8,9},{9,10},{10,1... | collective-permute-start | bytes 36872 | tf_op jit(solution)/shard_map/ppermute | solution.py:22
  20.6 4.6 %collective-permute-start.3 = (f32[12,2,128]{2,1,0:T(2,128)S(1)}, f32[12,2,128]{2,1,0:T(2,128)S(1)}, u32[]{:S(2)}, u32[]{:S(2)}) collective-permute-start(f32[12,2,128]{2,1,0:T(2,128)S(1)} %get-tuple-element.206), channel_id=1, source_target_pairs={{1,0},{2,1},{3,2},{4,3},{5,4},{6,5},{7,6},{8,7},{9,8},{10,9},{11,1... | collective-permute-start | bytes 36872 | tf_op jit(solution)/shard_map/ppermute | solution.py:24
  25.4 8.5 %collective-permute-start.5 = (f32[4,2,3,9,1,128]{5,3,4,2,1,0:T(8,128)S(1)}, f32[4,2,3,9,1,128]{5,3,4,2,1,0:T(8,128)S(1)}, u32[]{:S(2)}, u32[]{:S(2)}) collective-permute-start(f32[4,2,3,9,1,128]{5,3,4,2,1,0:T(8,128)S(1)} %copy.114), channel_id=1, source_target_pairs={{1,0},{2,1},{3,2},{4,3},{5,4},{6,5},{7,6},{8,7},{9,8},{10,9},{11,1... | collective-permute-start | bytes 331784 | tf_op jit(solution)/shard_map/ppermute | solution.py:34
  43.8 8.5 %copy-start.4 = (f32[24,24]{1,0:T(8,128)S(1)}, f32[24,24]{1,0:T(8,128)}, u32[]{:S(2)}) copy-start(f32[24,24]{1,0:T(8,128)} %param.13) | copy-start | bytes 6916
  68.3 4.8 %copy-start.10 = (f32[1,1,1,8,8,128]{5,4,3,2,1,0:T(8,128)S(1)}, f32[1,1,1,8,8,128]{5,4,3,2,1,0:T(8,128)}, u32[]{:S(2)}) copy-start(f32[1,1,1,8,8,128]{5,4,3,2,1,0:T(8,128)} %get-tuple-element.17) | copy-start | bytes 98308
  68.3 4.8 %copy-start.11 = (f32[1,1,1,8,8,128]{5,4,3,2,1,0:T(8,128)S(1)}, f32[1,1,1,8,8,128]{5,4,3,2,1,0:T(8,128)}, u32[]{:S(2)}) copy-start(f32[1,1,1,8,8,128]{5,4,3,2,1,0:T(8,128)} %get-tuple-element.18) | copy-start | bytes 98308
  68.3 4.8 %copy-start.12 = (f32[1,1,1,8,8,128]{5,4,3,2,1,0:T(8,128)S(1)}, f32[1,1,1,8,8,128]{5,4,3,2,1,0:T(8,128)}, u32[]{:S(2)}) copy-start(f32[1,1,1,8,8,128]{5,4,3,2,1,0:T(8,128)} %get-tuple-element.19) | copy-start | bytes 98308
  68.3 4.8 %copy-start.13 = (f32[1,1,1,8,8,128]{5,4,3,2,1,0:T(8,128)S(1)}, f32[1,1,1,8,8,128]{5,4,3,2,1,0:T(8,128)}, u32[]{:S(2)}) copy-start(f32[1,1,1,8,8,128]{5,4,3,2,1,0:T(8,128)} %get-tuple-element.20) | copy-start | bytes 98308
  68.4 4.8 %copy-start.14 = (f32[1,1,1,8,8,128]{5,4,3,2,1,0:T(8,128)S(1)}, f32[1,1,1,8,8,128]{5,4,3,2,1,0:T(8,128)}, u32[]{:S(2)}) copy-start(f32[1,1,1,8,8,128]{5,4,3,2,1,0:T(8,128)} %get-tuple-element.21) | copy-start | bytes 98308
  68.4 4.8 %copy-start.15 = (f32[1,1,1,8,8,128]{5,4,3,2,1,0:T(8,128)S(1)}, f32[1,1,1,8,8,128]{5,4,3,2,1,0:T(8,128)}, u32[]{:S(2)}) copy-start(f32[1,1,1,8,8,128]{5,4,3,2,1,0:T(8,128)} %get-tuple-element.22) | copy-start | bytes 98308
  68.4 4.8 %copy-start.16 = (f32[1,1,1,8,8,128]{5,4,3,2,1,0:T(8,128)S(1)}, f32[1,1,1,8,8,128]{5,4,3,2,1,0:T(8,128)}, u32[]{:S(2)}) copy-start(f32[1,1,1,8,8,128]{5,4,3,2,1,0:T(8,128)} %get-tuple-element.23) | copy-start | bytes 98308
  68.4 4.8 %copy-start.17 = (f32[1,1,1,8,8,128]{5,4,3,2,1,0:T(8,128)S(1)}, f32[1,1,1,8,8,128]{5,4,3,2,1,0:T(8,128)}, u32[]{:S(2)}) copy-start(f32[1,1,1,8,8,128]{5,4,3,2,1,0:T(8,128)} %get-tuple-element.24) | copy-start | bytes 98308
  68.4 4.8 %copy-start.18 = (f32[1,1,1,8,8,128]{5,4,3,2,1,0:T(8,128)S(1)}, f32[1,1,1,8,8,128]{5,4,3,2,1,0:T(8,128)}, u32[]{:S(2)}) copy-start(f32[1,1,1,8,8,128]{5,4,3,2,1,0:T(8,128)} %get-tuple-element.25) | copy-start | bytes 98308
  68.4 4.8 %copy-start.19 = (f32[1,1,1,8,8,128]{5,4,3,2,1,0:T(8,128)S(1)}, f32[1,1,1,8,8,128]{5,4,3,2,1,0:T(8,128)}, u32[]{:S(2)}) copy-start(f32[1,1,1,8,8,128]{5,4,3,2,1,0:T(8,128)} %get-tuple-element.26) | copy-start | bytes 98308
  68.4 4.8 %copy-start.20 = (f32[1,1,1,8,8,128]{5,4,3,2,1,0:T(8,128)S(1)}, f32[1,1,1,8,8,128]{5,4,3,2,1,0:T(8,128)}, u32[]{:S(2)}) copy-start(f32[1,1,1,8,8,128]{5,4,3,2,1,0:T(8,128)} %get-tuple-element.27) | copy-start | bytes 98308
  77.9 4.5 %copy-start.31 = (f32[1,1,1,8,8,128]{5,4,3,2,1,0:T(8,128)S(1)}, f32[1,1,1,8,8,128]{5,4,3,2,1,0:T(8,128)}, u32[]{:S(2)}) copy-start(f32[1,1,1,8,8,128]{5,4,3,2,1,0:T(8,128)} %get-tuple-element.194) | copy-start | bytes 98308
  77.9 4.5 %copy-start.32 = (f32[1,1,1,8,8,128]{5,4,3,2,1,0:T(8,128)S(1)}, f32[1,1,1,8,8,128]{5,4,3,2,1,0:T(8,128)}, u32[]{:S(2)}) copy-start(f32[1,1,1,8,8,128]{5,4,3,2,1,0:T(8,128)} %get-tuple-element.195) | copy-start | bytes 98308
  85.5 11.4 %copy-start.60 = (s32[1,64,1]{1,2,0:T(1,128)S(1)}, s32[1,64,1]{1,2,0:T(1,128)}, u32[]{:S(2)}) copy-start(s32[1,64,1]{1,2,0:T(1,128)} %broadcast_bitcast_fusion) | copy-start | bytes 772
  85.5 22.7 %copy-start.56 = (f32[63,64]{0,1:T(8,128)S(1)}, f32[63,64]{0,1:T(8,128)}, u32[]{:S(2)}) copy-start(f32[63,64]{0,1:T(8,128)} %constant.25.clone.1) | copy-start | bytes 48388
  86.8 10.1 %collective-permute-start.6 = (f32[2,8,128]{2,1,0:T(8,128)S(1)}, f32[2,8,128]{2,1,0:T(8,128)S(1)}, u32[]{:S(2)}, u32[]{:S(2)}) collective-permute-start(f32[2,8,128]{2,1,0:T(8,128)S(1)} %get-tuple-element.212), channel_id=1, source_target_pairs={{0,16},{16,32},{32,48},{48,64},{64,80},{80,96},{96,112},{112,128},... | collective-permute-start | bytes 24584 | tf_op jit(solution)/shard_map/ppermute | solution.py:22
  94.9 8.9 %collective-permute-start.7 = (f32[2,8,128]{2,1,0:T(8,128)S(1)}, f32[2,8,128]{2,1,0:T(8,128)S(1)}, u32[]{:S(2)}, u32[]{:S(2)}) collective-permute-start(f32[2,8,128]{2,1,0:T(8,128)S(1)} %get-tuple-element.213), channel_id=1, source_target_pairs={{16,0},{32,16},{48,32},{64,48},{80,64},{96,80},{112,96},{128,112},... | collective-permute-start | bytes 24584 | tf_op jit(solution)/shard_map/ppermute | solution.py:24
  103.8 4.6 %collective-permute-start.8 = (f32[12,2,128]{2,1,0:T(2,128)S(1)}, f32[12,2,128]{2,1,0:T(2,128)S(1)}, u32[]{:S(2)}, u32[]{:S(2)}) collective-permute-start(f32[12,2,128]{2,1,0:T(2,128)S(1)} %get-tuple-element.203), channel_id=1, source_target_pairs={{0,1},{1,2},{2,3},{3,4},{4,5},{5,6},{6,7},{7,8},{8,9},{9,10},{10,1... | collective-permute-start | bytes 36872 | tf_op jit(solution)/shard_map/ppermute | solution.py:22
  106.9 7.1 %collective-permute-start.9 = (f32[12,2,128]{2,1,0:T(2,128)S(1)}, f32[12,2,128]{2,1,0:T(2,128)S(1)}, u32[]{:S(2)}, u32[]{:S(2)}) collective-permute-start(f32[12,2,128]{2,1,0:T(2,128)S(1)} %get-tuple-element.204), channel_id=1, source_target_pairs={{1,0},{2,1},{3,2},{4,3},{5,4},{6,5},{7,6},{8,7},{9,8},{10,9},{11,1... | collective-permute-start | bytes 36872 | tf_op jit(solution)/shard_map/ppermute | solution.py:24
  108.4 6.5 %copy-start.57 = (f32[8,8,128]{2,1,0:T(8,128)S(1)}, f32[8,8,128]{2,1,0:T(8,128)}, u32[]{:S(2)}) copy-start(f32[8,8,128]{2,1,0:T(8,128)} %get-tuple-element.207) | copy-start | bytes 98308
  108.4 6.5 %copy-start.58 = (f32[8,8,128]{2,1,0:T(8,128)S(1)}, f32[8,8,128]{2,1,0:T(8,128)}, u32[]{:S(2)}) copy-start(f32[8,8,128]{2,1,0:T(8,128)} %get-tuple-element.208) | copy-start | bytes 98308
  114.3 114.4 %copy-start.59 = (f32[64]{0:T(128)S(1)}, f32[64]{0:T(128)}, u32[]{:S(2)}) copy-start(f32[64]{0:T(128)} %param.15) | copy-start | bytes 772
  114.8 118.4 %copy-start.30 = (f32[8,8,128]{2,1,0:T(8,128)}, f32[8,8,128]{2,1,0:T(8,128)S(1)}, u32[]{:S(2)}) copy-start(f32[8,8,128]{2,1,0:T(8,128)S(1)} %get-tuple-element.6) | copy-start | bytes 98308
  (39 other events, 111.5 us)
where the time goes:
time: 236 us; the launch traced here: 234 us
  blocking collectives  112 us (47%)
  local copies, waits for them, and re-layouts  46.5 us (20%)
  starting transfers between devices  32.5 us (14%)
  waiting for transfers between devices  20.3 us (9%)
  matrix products  11.7 us (5%)
  other arithmetic  9.3 us (4%)
    psum x1, blocking collectives, bisect_round(): volumes = lax.psum(partial_volumes, ('gx', 'gy'))  112 us
    another operation x8, local copies, waits for them, and re-layouts, element_terms(): vectors.append(jnp.stack(row_list))  31 us
    ppermute x4, starting transfers between devices, with_halo(): lax.ppermute(tail, axis, [(i, (i + 1) % count) for i in range(ends)])  15.6 us
    ppermute x4, waiting for transfers between devices, with_halo(): lax.ppermute(head, axis, [((i + 1) % count, i) for i in range(ends)])  15.3 us
    ppermute x4, starting transfers between devices, with_halo(): lax.ppermute(head, axis, [((i + 1) % count, i) for i in range(ends)])  13.3 us
    slice x9, local copies, waits for them, and re-layouts, element_terms(): extended[pair_index, member, component, corner_x:corner_x + cells_x, corn...  8.41 us
    dot_general x4, matrix products, element_terms(): jnp.dot(mass_matrix, adjoint_rows, precision=lax.Precision.HIGHEST)  7.02 us
    ppermute x2, waiting for transfers between devices, from_behind(): lax.ppermute(value, axis, [(source, source + steps) for source in range(i...  4.95 us
  transfers between devices with their start and end apart: 10, of which 4 were waited for; matrix products, arithmetic and copies ran while one was open for 3% of the time, Pallas kernels for 0%

commit v1 on v0

--- a/solution.py
+++ b/solution.py
@@ -173,7 +173,7 @@
         partial_volumes = (
             jnp.sum(fields_of, axis=(1, 2)).reshape(len(midpoints), REGIONS, band_cells).sum(axis=2)
         )
-        volumes = lax.psum(partial_volumes, ("gx", "gy"))
+        volumes = jnp.sum(lax.all_gather(partial_volumes, ("gx", "gy")), axis=0)
         position = jnp.zeros((REGIONS,), jnp.int32)
         for depth in range(levels):
             middle = jnp.sqrt(low_end * high_end)

time: 236 us -> 1580 us (6.69)
  waiting for transfers between devices: 20.3 us -> 1460 us
  blocking collectives: 112 us -> 0 us
    all_gather x0 -> x1, waiting for transfers between devices: none -> 1450 us  [bisect_round(): volumes = jnp.sum(lax.all_gather(partial_volumes, ('gx', 'gy')), axis=0)]
    psum x1 -> x0, blocking collectives: 112 us -> none  [bisect_round(): volumes = lax.psum(partial_volumes, ('gx', 'gy'))]
  transfers between devices with their start and end apart: 10 -> 11, of which waited for: 4 -> 6; matrix products, arithmetic and copies ran while one was open for 3% -> 0% of each run, Pallas kernels for 0% -> 0%
where the time goes in v1:
time: 1580 us
  waiting for transfers between devices  1460 us (92%)
  local copies, waits for them, and re-layouts  40.1 us (3%)
  starting transfers between devices  34.6 us (2%)
  other arithmetic  17 us (1%)
    all_gather x1, waiting for transfers between devices, bisect_round(): volumes = jnp.sum(lax.all_gather(partial_volumes, ('gx', 'gy')), axis=0)  1450 us
  transfers between devices with their start and end apart: 11, of which 6 were waited for; matrix products, arithmetic and copies ran while one was open for 0% of the time, Pallas kernels for 0%

profile of v1, /device:TPU:1, one launch (start us, length us, event | category | flops | bytes accessed | tf_op | source)
XLA Modules:
  0.0 1575.3 jit_solution(17115776771104146260)
XLA Ops:
  7.9 8.8 collective-permute-start
  16.8 1.9 collective-permute-start.1
  19.5 1.2 broadcast_multiply_fusion
  20.7 1.9 collective-permute-start.4
  23.5 1.4 add_minimum_fusion
  25.7 1.3 collective-permute-start.3
  27.0 4.0 collective-permute-start.2
  32.1 1.3 collective-permute-start.5
  35.6 4.2 collective-permute-done.5
  44.6 1.0 pad_slice_fusion.79
  45.6 0.9 pad_slice_fusion.48
  46.5 1.1 stack.30
  47.6 3.7 stack.31
  51.4 1.5 fusion.20
  52.9 1.5 fusion.16
  54.3 3.6 stack.28
  58.0 3.5 stack.29
  61.5 1.5 fusion.19
  63.0 1.5 fusion.15
  64.5 3.7 stack.24
  68.3 3.9 stack.25
  73.9 3.5 stack.26
  77.5 2.8 stack.27
  82.0 1.2 fusion.98
  83.3 1.9 collective-permute-start.7
  85.2 8.5 collective-permute-start.6
  94.6 3.4 collective-permute-start.8
  97.9 1.5 collective-permute-start.9
  99.6 2.8 collective-permute-done.9
  103.1 0.9 fusion.12
  105.1 1450.3 %all-gather.4.cloned.1.call-done = f32[512,63,64]{2,1,0:T(8,128)} async-done(((f32[1,63,64]{2,1,0:T(8,128)}), f32[512,63,64]{2,1,0:T(8,128)}) %all-gather.4.cloned.1.call-update) | async-done | bytes 8257552 | tf_op jit(solution)/shard_map/all_gather | solution.py:176
  1555.4 7.0 reduce_sum.109
  (115 shorter events, 23.2 us)
Async XLA Ops:
  7.2 44.2 %copy-start = (f32[24,24]{1,0:T(8,128)S(1)}, f32[24,24]{1,0:T(8,128)}, u32[]{:S(2)}) copy-start(f32[24,24]{1,0:T(8,128)} %param.14) | copy-start | bytes 6916
  7.2 1548.2 %all-gather.4.cloned.1.call-start = ((), (), s32[]{:S(2)}) async-start(), calls=%async_computation | async-start | bytes 16809984 | tf_op jit(solution)/shard_map/all_gather | solution.py:176
  7.9 15.6 collective-permute-start
  16.8 8.9 collective-permute-start.1
  20.7 11.3 collective-permute-start.4
  25.7 5.4 collective-permute-start.3
  27.0 4.8 collective-permute-start.2
  32.1 7.7 collective-permute-start.5
  45.6 7.3 copy-start.2
  58.0 10.2 copy-start.7
  58.0 10.2 copy-start.8
  58.0 10.2 copy-start.9
  64.5 9.4 copy-start.3
  64.5 9.4 copy-start.4
  73.8 8.1 copy-start.1
  73.9 8.1 copy-start.5
  73.9 8.1 copy-start.6
  73.9 8.1 copy-start.10
  73.9 8.1 copy-start.11
  73.9 8.1 copy-start.13
  81.1 18.4 %copy-start.14 = (f32[63,64]{0,1:T(8,128)S(1)}, f32[63,64]{0,1:T(8,128)}, u32[]{:S(2)}) copy-start(f32[63,64]{0,1:T(8,128)} %constant.25.clone.1) | copy-start | bytes 48388
  82.0 21.1 %copy-start.15 = (f32[8,8,128]{2,1,0:T(8,128)S(1)}, f32[8,8,128]{2,1,0:T(8,128)}, u32[]{:S(2)}) copy-start(f32[8,8,128]{2,1,0:T(8,128)} %get-tuple-element.207) | copy-start | bytes 98308
  82.0 21.1 %copy-start.16 = (f32[8,8,128]{2,1,0:T(8,128)S(1)}, f32[8,8,128]{2,1,0:T(8,128)}, u32[]{:S(2)}) copy-start(f32[8,8,128]{2,1,0:T(8,128)} %get-tuple-element.208) | copy-start | bytes 98308
  83.3 10.5 collective-permute-start.7
  85.2 9.3 collective-permute-start.6
  94.6 5.0 collective-permute-start.8
  97.9 4.4 collective-permute-start.9
  103.1 1464.7 %copy-start.12 = (f32[8,8,128]{2,1,0:T(8,128)}, f32[8,8,128]{2,1,0:T(8,128)S(1)}, u32[]{:S(2)}) copy-start(f32[8,8,128]{2,1,0:T(8,128)S(1)} %get-tuple-element.6) | copy-start | bytes 98308
  105.1 1458.2 %copy-start.17 = (f32[64]{0:T(128)S(1)}, f32[64]{0:T(128)}, u32[]{:S(2)}) copy-start(f32[64]{0:T(128)} %param.15) | copy-start | bytes 772
Sparse Core Ops, SparseCore 0:
  105.1 1450.2 all-gather.3
